TPU v7x, 256 devices: a whole 4x4x8 slice. The times are simulated.
256 devices in a mesh: sec: 2 (over y_lo), dp: 8 (over x, y_hi), seq: 16 (over z, core).
Axes of the slice: x: 4, y: 4 (y_hi: 2, y_lo: 2; y = y_hi * 2 + y_lo), z: 8, core: 2. Of those that a mesh axis runs over, the one named last changes fastest.
Arguments:
- hidden: bfloat16 [256, 128, 2560], P(('sec', 'dp', 'seq')), may hold values from -24 to 24
- cond_shift: bfloat16 [256, 2560], P(('sec', 'dp', 'seq')), may hold values from -0.3125 to 0.3125
- cond_scale: bfloat16 [256, 2560], P(('sec', 'dp', 'seq')), may hold values from -1.75 to 1.75
- noisy: bfloat16 [256, 128, 256], P(('sec', 'dp', 'seq')), may hold values from -6 to 6
- noise_level: float32 [256], P(('sec', 'dp', 'seq')), may hold values from 0.2 to 1
- w_out: bfloat16 [2560, 256], replicated, may hold values from -0.125 to 0.125
- w_embed: bfloat16 [256, 2048], replicated, may hold values from -0.375 to 0.375
- w_root: bfloat16 [2, 2048], replicated, may hold values from -0.03125 to 0.03125
- w_qkv: bfloat16 [3, 2048, 2048], P(None, None, 'seq'), may hold values from -0.125 to 0.125
- w_proj: bfloat16 [2048, 512], P('seq'), may hold values from -0.125 to 0.125
- text_table: bfloat16 [49408, 512], P('seq'), may hold values from -6 to 6
- text_ids: int32 [32, 32], replicated, may hold values from 0 to 49407
- prompt_index: int32 [256], P(('sec', 'dp')), may hold values from 0 to 31
- reward_weight: float32 [256], P(('sec', 'dp')), may hold values from 1000 to 4000
Outputs:
- rewards: float32 [256], P(('sec', 'dp'))
- grad_w_out: float32 [2560, 256], P('seq')
- grad_hidden: bfloat16 [256, 128, 2560], P(('sec', 'dp', 'seq'))
All inputs are finite; a program needn't handle non-finite values.
Results may differ from a plain program's by a relative error of at most 0.017.
The roundings to bfloat16 on the way count: a program that leaves them out, or rounds other values in their place, can miss the bound.
Values may be sent and summed in bfloat16 or wider, within the bound.
No kernel may reach another device: no remote copies, remote signals or barrier semaphores. Data moves between devices by JAX's collectives and lax.ppermute only.
A program may use at most 128 MiB of HBM per device.

v0:
```python
import jax
import jax.numpy as jnp
from jax import lax
from jax.sharding import PartitionSpec as P

D_REW = 2048
HEADS = 16
PROMPTS = 32
normalizing_sharpness = 10.0
epsilon = 1e-06
highest = lax.Precision.HIGHEST


def rotate(angle, first, second):
    cosine = jnp.cos(angle)
    sine_term = jnp.sin(angle)
    return (cosine * first + sine_term * second, cosine * second - sine_term * first)


def suffix(values):
    return jnp.sum(values, axis=1, keepdims=True) - jnp.cumsum(values, axis=1)


def local_path(motion):
    spin = motion[..., 0]
    theta = jnp.cumsum(spin, axis=1) - spin
    step_east, step_north = rotate(theta, motion[..., 1], motion[..., 2])
    path_east = jnp.cumsum(step_east, axis=1) - step_east
    path_north = jnp.cumsum(step_north, axis=1) - step_north
    return (theta, path_east, path_north)


def embed(motion, root_east, root_north, w_embed, root_rows):
    emb = jnp.einsum(
        "cfe,ed->cfd", motion.astype(jnp.bfloat16), w_embed, preferred_element_type=jnp.float32
    )
    emb = emb + root_east[..., None] * root_rows[0] + root_north[..., None] * root_rows[1]
    scale_rms = jnp.sqrt(jnp.mean(emb * emb, axis=-1, keepdims=True) + epsilon)
    return (emb / scale_rms, scale_rms)


def unit_rows(vectors):
    length = jnp.sqrt(jnp.sum(vectors * vectors, axis=-1, keepdims=True) + epsilon)
    return (vectors / length, length)


def norm_grad(grad, normed, scale_rms):
    return (grad - normed * jnp.mean(grad * normed, axis=-1, keepdims=True)) / scale_rms


def motion_grad(d_emb, normed_e, scale_rms, motion, theta, embed_rows, root_rows):
    d_unemb = norm_grad(d_emb, normed_e, scale_rms)
    d_embedded = jnp.einsum("cfd,ed->cfe", d_unemb, embed_rows, precision=highest)
    grad_east = suffix(jnp.sum(d_unemb * root_rows[0], axis=-1))
    grad_north = suffix(jnp.sum(d_unemb * root_rows[1], axis=-1))
    vel_east = motion[..., 1]
    vel_north = motion[..., 2]
    d_east, d_north = rotate(-theta, grad_east, grad_north)
    cosine = jnp.cos(theta)
    sine_term = jnp.sin(theta)
    d_theta = grad_east * (cosine * vel_north - sine_term * vel_east) - grad_north * (
        cosine * vel_east + sine_term * vel_north
    )
    d_spin = suffix(d_theta)
    return d_embedded.at[..., 0].add(d_spin).at[..., 1].add(d_east).at[..., 2].add(d_north)


def local(
    hidden,
    cond_shift,
    cond_scale,
    noisy,
    noise_level,
    w_out,
    w_embed,
    w_root,
    w_qkv,
    w_proj,
    text_table,
    text_ids,
    prompt_index,
    reward_weight,
):
    clips_dev = hidden.shape[0]
    ways = lax.axis_size("seq")
    group = clips_dev * ways
    frames = hidden.shape[1]
    width_cols = w_qkv.shape[2]
    head_size = D_REW // HEADS
    heads_dev = width_cols // head_size
    root_rows = w_root.astype(jnp.float32)
    embed_rows = w_embed.astype(jnp.float32)
    vocab_rows = text_table.shape[0]
    local_ids = text_ids - lax.axis_index("seq") * vocab_rows
    inside = (local_ids >= 0) & (local_ids < vocab_rows)
    picked = jnp.take(text_table, jnp.clip(local_ids, 0, vocab_rows - 1), axis=0).astype(
        jnp.float32
    )
    text_part = jnp.sum(jnp.where(inside[..., None], picked, 0.0), axis=1)
    text_raw = lax.psum(text_part, "seq")
    text_unit, text_len = unit_rows(text_raw)
    hidden_f = hidden.astype(jnp.float32)
    centred = hidden_f - jnp.mean(hidden_f, axis=-1, keepdims=True)
    inv_std = lax.rsqrt(jnp.mean(centred * centred, axis=-1, keepdims=True) + epsilon)
    normed_h = centred * inv_std
    gain = 1.0 + cond_scale.astype(jnp.float32)[:, None, :]
    modulated = (normed_h * gain + cond_shift.astype(jnp.float32)[:, None, :]).astype(jnp.bfloat16)
    eps_pred = jnp.einsum("cfd,de->cfe", modulated, w_out, preferred_element_type=jnp.float32)
    level = noise_level[:, None, None]
    x_clean = noisy.astype(jnp.float32) - level * eps_pred
    theta, path_east, path_north = local_path(x_clean)
    normed_e, scale_rms = embed(x_clean, path_east, path_north, w_embed, root_rows)
    projected = jnp.einsum(
        "cfd,jdk->cfjk",
        lax.all_gather(normed_e.astype(jnp.bfloat16), "seq", axis=0, tiled=True),
        w_qkv,
        preferred_element_type=jnp.float32,
    )
    projected = projected.reshape(group, frames, 3, heads_dev, head_size)
    query_unit, query_len = unit_rows(projected[:, :, 0])
    key_unit, key_len = unit_rows(projected[:, :, 1])
    asking_vectors_group = query_unit.astype(jnp.bfloat16)
    lookup_vectors_group = key_unit.astype(jnp.bfloat16)
    value_b = projected[:, :, 2].astype(jnp.bfloat16)
    similarity_table = normalizing_sharpness * jnp.einsum(
        "cfhd,cghd->chfg",
        asking_vectors_group,
        lookup_vectors_group,
        preferred_element_type=jnp.float32,
    )
    expo = jnp.exp(similarity_table)
    focus_probabilities = expo / jnp.sum(expo, axis=-1, keepdims=True)
    attention_b = focus_probabilities.astype(jnp.bfloat16)
    column_mass = jnp.sum(attention_b, axis=2, dtype=jnp.float32)
    value_f = value_b.astype(jnp.float32)
    pooled = jnp.einsum("chg,cghd->chd", column_mass, value_f, precision=highest)
    pooled_b = pooled.astype(jnp.bfloat16).reshape(group, width_cols)
    motion_part = jnp.dot(pooled_b, w_proj, preferred_element_type=jnp.float32)
    motion_emb = lax.psum(motion_part, "seq")
    choose = (prompt_index[:, None] == jnp.arange(PROMPTS)[None, :]).astype(jnp.float32)
    target = jnp.dot(choose, text_unit, precision=highest)
    emb_len = jnp.sqrt(jnp.sum(motion_emb * motion_emb, axis=-1) + epsilon)
    rewards = jnp.sum(motion_emb * target, axis=-1) / emb_len
    d_memb = (
        (-reward_weight)[:, None]
        * (target - rewards[:, None] * motion_emb / emb_len[:, None])
        / emb_len[:, None]
    )
    d_pooled = jnp.dot(d_memb, w_proj.astype(jnp.float32).T, precision=highest).reshape(
        group, heads_dev, head_size
    )
    reduction_dimension = jnp.einsum("chd,cghd->chg", d_pooled, value_f, precision=highest)
    d_value = jnp.transpose(column_mass, (0, 2, 1))[..., None] * d_pooled[:, None]
    pairwise_dot_similarity = jnp.sum(
        focus_probabilities * reduction_dimension[:, :, None, :], axis=-1, keepdims=True
    )
    similarity_derivative = (
        normalizing_sharpness
        * focus_probabilities
        * (reduction_dimension[:, :, None, :] - pairwise_dot_similarity)
    ).astype(jnp.bfloat16)
    d_qu = jnp.einsum(
        "chfg,cghd->cfhd",
        similarity_derivative,
        lookup_vectors_group,
        preferred_element_type=jnp.float32,
    )
    d_ku = jnp.einsum(
        "chfg,cfhd->cghd",
        similarity_derivative,
        asking_vectors_group,
        preferred_element_type=jnp.float32,
    )
    d_query = (d_qu - query_unit * jnp.sum(query_unit * d_qu, axis=-1, keepdims=True)) / query_len
    d_key = (d_ku - key_unit * jnp.sum(key_unit * d_ku, axis=-1, keepdims=True)) / key_len
    d_proj = (
        jnp.stack([d_query, d_key, d_value], axis=2)
        .astype(jnp.bfloat16)
        .reshape(group, frames, 3, width_cols)
    )
    d_emb = lax.psum_scatter(
        jnp.einsum("cfjk,jdk->cfd", d_proj, w_qkv, preferred_element_type=jnp.float32),
        "seq",
        scatter_dimension=0,
        tiled=True,
    )
    d_motion = motion_grad(d_emb, normed_e, scale_rms, x_clean, theta, embed_rows, root_rows)
    d_eps_b = (-level * d_motion).astype(jnp.bfloat16)
    d_mod = jnp.einsum("cfe,de->cfd", d_eps_b, w_out, preferred_element_type=jnp.float32)
    d_norm = d_mod * gain
    grad_hidden = (
        inv_std
        * (
            d_norm
            - jnp.mean(d_norm, axis=-1, keepdims=True)
            - normed_h * jnp.mean(d_norm * normed_h, axis=-1, keepdims=True)
        )
    ).astype(jnp.bfloat16)
    rows_dev = w_out.shape[0] // ways
    grad_term = jnp.einsum("cfd,cfe->de", modulated, d_eps_b, preferred_element_type=jnp.float32)
    grad_total = lax.psum(grad_term, ("sec", "dp", "seq"))
    grad_w_out = lax.dynamic_slice_in_dim(grad_total, lax.axis_index("seq") * rows_dev, rows_dev, 0)
    return (rewards, grad_w_out, grad_hidden)


def solution(mesh):
    placed = (
        P(("sec", "dp", "seq"), None, None),
        P(("sec", "dp", "seq"), None),
        P(("sec", "dp", "seq"), None),
        P(("sec", "dp", "seq"), None, None),
        P(("sec", "dp", "seq")),
        P(),
        P(),
        P(),
        P(None, None, "seq"),
        P("seq", None),
        P("seq", None),
        P(),
        P(("sec", "dp")),
        P(("sec", "dp")),
    )
    return jax.shard_map(
        local,
        mesh=mesh,
        in_specs=placed,
        out_specs=(P(("sec", "dp")), P("seq", None), P(("sec", "dp", "seq"), None, None)),
        check_vma=False,
    )
```

profile of v0, /device:TPU:2, one launch (start us, length us, event | category | flops | bytes accessed | tf_op | source)
XLA Modules:
  0.0 640.3 jit_solution(5430359469314224564)
XLA Ops:
  9.1 5.1 gather_fusion
  14.2 2.3 select_reduce_fusion
  17.3 1.3 convert_reduce_fusion
  18.5 1.4 fusion.22
  20.7 1.8 fusion.24
  26.0 1.7 multiply_reduce_fusion.3
  30.3 88.0 %all-reduce.3.cloned.1.call-done = f32[32,512]{1,0:T(8,128)} async-done(((f32[32,512]{1,0:T(8,128)}), f32[32,512]{1,0:T(8,128)}) %all-reduce.3.cloned.1.call-update) | async-done | bytes 65552 | tf_op jit(solution)/shard_map/psum | solution.py:100
  118.3 1.0 multiply_reduce_fusion.8
  119.8 55.7 %all-gather.3.cloned.1.call-done = bf16[2048,2048]{1,0:T(8,128)(2,1)} async-done(((bf16[128,2048]{1,0:T(8,128)(2,1)}), bf16[2048,2048]{1,0:T(8,128)(2,1)}) %all-gather.3.cloned.1.call-update) | async-done | bytes 8388624 | tf_op jit(solution)/shard_map/all_gather | solution.py:115
  175.5 6.4 convolution_bitcast_fusion.1
  182.1 1.6 fusion.32
  183.9 2.7 convert_reduce_fusion.1
  186.6 2.1 fusion.37
  188.8 47.4 %psum.21 = f32[16,512]{1,0:T(8,128)} all-reduce(f32[16,512]{1,0:T(8,128)S(1)} %fusion.59), channel_id=1, replica_groups=mesh['sec'=2,'dp'=8,'seq'=16] {'seq'}, use_global_device_ids=true, to_apply=%region_10.11 | all-reduce | flops 8192 | bytes 65536 | tf_op jit(solution)/shard_map/psum | solution.py:139
  236.2 1.2 multiply_reduce_fusion.9
  237.5 1.0 fusion.45
  238.8 1.7 fusion.35
  241.5 1.0 copy-done.2
  244.8 8.1 %convolution_bitcast_fusion = f32[16,128,2048]{2,1,0:T(8,128)} fusion(bf16[16,128,1,128]{1,3,0,2:T(8,128)(2,1)S(1)} %multiply_convert_fusion, bf16[16,128,1,128]{1,3,0,2:T(8,128)(2,1)S(1)} %get-tuple-element.60, bf16[16,128,1,128]{1,3,0,2:T(8,128)(2,1)S(1)} %get-tuple-element.59, bf16[3,2048,128]{2,1,0:T(8,128)(2,1)S(1)} %copy-done.9), kind=kOutput, calls=%fused_computation.2 | convolution fusion | flops 3222798336 | bytes 19922944 | tf_op jit(solution)/shard_map/cfjk,jdk->cfd/dot_general | solution.py:182
  253.2 100.2 %reduce-scatter.2.cloned.1.call-done = f32[1,128,2048]{2,1,0:T(8,128)} async-done(((f32[16,128,2048]{2,1,0:T(8,128)}), f32[1,128,2048]{2,1,0:T(8,128)}) %reduce-scatter.2.cloned.1.call-update) | async-done | bytes 1048592 | tf_op jit(solution)/shard_map/reduce_scatter | solution.py:181
  353.5 1.9 fusion.30
  355.7 2.1 multiply_reduce_fusion.7
  358.4 2.0 fusion.66
  360.8 2.7 fusion.27
  363.6 1.3 fusion.40
  364.9 1.0 scatter-add.10
  367.2 3.3 fusion.53
  371.2 3.2 fusion.18
  374.3 1.5 reduce_sum.224
  375.8 2.8 fusion.21
  378.7 253.5 %all-reduce.5.cloned.1.call-done = f32[2560,256]{1,0:T(8,128)} async-done(((f32[2560,256]{1,0:T(8,128)}), f32[2560,256]{1,0:T(8,128)}) %all-reduce.5.cloned.1.call-update) | async-done | bytes 2621456 | tf_op jit(solution)/shard_map/psum | solution.py:201
  632.2 1.6 constant_dynamic-slice_fusion
  (126 shorter events, 16.8 us)
Async XLA Ops:
  7.2 1.9 copy-start
  7.2 111.1 %all-reduce.3.cloned.1.call-start = ((), (), s32[]{:S(2)}) async-start(), calls=%async_computation.1 | async-start | bytes 131072 | tf_op jit(solution)/shard_map/psum | solution.py:100
  14.1 5.8 copy-start.20
  14.1 6.4 %copy-start.21 = (bf16[1,2560]{1,0:T(2,128)(2,1)S(1)}, bf16[1,2560]{1,0:T(2,128)(2,1)}, u32[]{:S(2)}) copy-start(bf16[1,2560]{1,0:T(2,128)(2,1)} %param.21) | copy-start | bytes 15364
  14.1 6.4 %copy-start.22 = (bf16[1,2560]{1,0:T(2,128)(2,1)S(1)}, bf16[1,2560]{1,0:T(2,128)(2,1)}, u32[]{:S(2)}) copy-start(bf16[1,2560]{1,0:T(2,128)(2,1)} %param.22) | copy-start | bytes 15364
  14.2 6.5 %copy-start.36 = (bf16[1,128,256]{2,1,0:T(8,128)(2,1)S(1)}, bf16[1,128,256]{2,1,0:T(8,128)(2,1)}, u32[]{:S(2)}) copy-start(bf16[1,128,256]{2,1,0:T(8,128)(2,1)} %param.23) | copy-start | bytes 196612
  16.5 159.0 %all-gather.3.cloned.1.call-start = ((), (), s32[]{:S(2)}) async-start(), calls=%async_computation.4 | async-start | bytes 8912896 | tf_op jit(solution)/shard_map/all_gather | solution.py:115
  16.5 4.1 copy-start.3
  18.5 3.9 copy-start.23
  20.0 2.5 copy-start.27
  20.7 1.8 copy-start.14
  24.9 2.8 copy-start.10
  27.8 2.0 copy-start.37
  29.7 323.8 %reduce-scatter.2.cloned.1.call-start = ((), (), s32[]{:S(2)}) async-start(), calls=%async_computation.2 | async-start | bytes 17825792 | tf_op jit(solution)/shard_map/reduce_scatter | solution.py:181
  181.9 2.0 copy-start.1
  183.9 4.8 copy-start.13
  183.9 52.3 %copy-start.16 = (f32[32,512]{1,0:T(8,128)S(1)}, f32[32,512]{1,0:T(8,128)}, u32[]{:S(2)}) copy-start(f32[32,512]{1,0:T(8,128)} %all-reduce.3.cloned.1.call-done) | copy-start | bytes 196612
  236.2 4.4 copy-start.6
  237.4 3.5 copy-start.35
  238.4 2.5 copy-start.8
  240.6 1.9 copy-start.2
  253.0 100.5 %copy-start.26 = (f32[128]{0:T(128)S(1)}, f32[128]{0:T(128)}, u32[]{:S(2)}) copy-start(f32[128]{0:T(128)} %copy-done.25) | copy-start | bytes 1540
  253.0 102.5 %copy-start.19 = (f32[1,2048]{1,0:T(1,128)S(1)}, f32[1,2048]{1,0:T(1,128)}, u32[]{:S(2)}) copy-start(f32[1,2048]{1,0:T(1,128)} %get-tuple-element.67) | copy-start | bytes 24580
  253.0 102.5 %copy-start.18 = (f32[1,2048]{1,0:T(1,128)S(1)}, f32[1,2048]{1,0:T(1,128)}, u32[]{:S(2)}) copy-start(f32[1,2048]{1,0:T(1,128)} %get-tuple-element.66) | copy-start | bytes 24580
  253.0 379.2 %all-reduce.5.cloned.1.call-start = ((), (), s32[]{:S(2)}) async-start(), calls=%async_computation.3 | async-start | bytes 5242880 | tf_op jit(solution)/shard_map/psum | solution.py:201
  353.5 2.0 copy-start.5
  353.5 2.2 copy-start.7
  355.6 2.7 copy-start.29
  355.6 2.7 copy-start.30
  355.6 2.7 copy-start.32
  355.6 2.7 copy-start.34
  355.6 5.0 copy-start.11
  (10 other events, 10.1 us)
Sparse Core Ops, SparseCore 0:
  16.6 101.6 all-reduce.2
  120.9 54.6 all-gather.2
  253.1 100.3 reduce-scatter.1
  370.6 261.4 all-reduce.4
where the time goes:
time: 641 us; the launch traced here: 640 us
  waiting for transfers between devices  498 us (78%)
  blocking collectives  47.4 us (7%)
  matrix products  37.3 us (6%)
  other arithmetic  26.9 us (4%)
  local copies, waits for them, and re-layouts  15.9 us (2%)
  between operations  14.9 us (2%)
    psum x1, waiting for transfers between devices, local(): grad_total = lax.psum(grad_term, ('sec', 'dp', 'seq'))  253 us
    reduce_scatter x1, waiting for transfers between devices, local(): lax.psum_scatter(jnp.einsum('cfjk,jdk->cfd', d_proj, w_qkv, preferred_ele...  100 us
    psum x1, waiting for transfers between devices, local(): text_raw = lax.psum(text_part, 'seq')  88 us
    all_gather x1, waiting for transfers between devices, local(): lax.all_gather(normed_e.astype(jnp.bfloat16), 'seq', axis=0, tiled=True)  55.7 us
    psum x1, blocking collectives, local(): motion_emb = lax.psum(motion_part, 'seq')  47.4 us
  transfers between devices with their start and end apart: 4, of which 4 were waited for; matrix products, arithmetic and copies ran while one was open for 3% of the time, Pallas kernels for 0%

commit v1 on v0

--- a/solution.py
+++ b/solution.py
@@ -9,6 +9,11 @@
 normalizing_sharpness = 10.0
 epsilon = 1e-06
 highest = lax.Precision.HIGHEST
+
+
+def by_each_axis(value, leading, second_2):
+    partial = lax.psum(value, leading)
+    return lax.psum(partial, second_2)
 
 
 def rotate(angle, first, second):
@@ -198,7 +203,7 @@
     ).astype(jnp.bfloat16)
     rows_dev = w_out.shape[0] // ways
     grad_term = jnp.einsum("cfd,cfe->de", modulated, d_eps_b, preferred_element_type=jnp.float32)
-    grad_total = lax.psum(grad_term, ("sec", "dp", "seq"))
+    grad_total = by_each_axis(grad_term, ("dp", "seq"), "sec")
     grad_w_out = lax.dynamic_slice_in_dim(grad_total, lax.axis_index("seq") * rows_dev, rows_dev, 0)
     return (rewards, grad_w_out, grad_hidden)
 

time: 641 us -> 1710 us (2.67)
  waiting for transfers between devices: 498 us -> 1560 us
    psum x1 -> x2, waiting for transfers between devices: 253 us -> 1320 us  [the longest x1 1180 us: by_each_axis(): partial = lax.psum(value, leading)]
  transfers between devices with their start and end apart: 4 -> 5, of which waited for: 4 -> 5; matrix products, arithmetic and copies ran while one was open for 3% -> 1% of each run, Pallas kernels for 0% -> 0%
where the time goes in v1:
time: 1710 us; the launch traced here: 1700 us
  waiting for transfers between devices  1560 us (91%)
  blocking collectives  47.4 us (3%)
  matrix products  37.3 us (2%)
  other arithmetic  26.9 us (2%)
    psum x1, waiting for transfers between devices, by_each_axis(): partial = lax.psum(value, leading)  1180 us
    psum x1, waiting for transfers between devices, by_each_axis(): return lax.psum(partial, second_2)  143 us
    reduce_scatter x1, waiting for transfers between devices, local(): lax.psum_scatter(jnp.einsum('cfjk,jdk->cfd', d_proj, w_qkv, preferred_ele...  100 us
    psum x1, waiting for transfers between devices, local(): text_raw = lax.psum(text_part, 'seq')  88 us
    all_gather x1, waiting for transfers between devices, local(): lax.all_gather(normed_e.astype(jnp.bfloat16), 'seq', axis=0, tiled=True)  55.7 us
    psum x1, blocking collectives, local(): motion_emb = lax.psum(motion_part, 'seq')  47.4 us
  transfers between devices with their start and end apart: 5, of which 5 were waited for; matrix products, arithmetic and copies ran while one was open for 1% of the time, Pallas kernels for 0%

profile of v1, /device:TPU:2, one launch (start us, length us, event | category | flops | bytes accessed | tf_op | source)
XLA Modules:
  0.0 1704.8 jit_solution(3453274820020587486)
XLA Ops:
  9.1 5.1 gather_fusion
  14.2 2.3 select_reduce_fusion
  17.3 1.3 convert_reduce_fusion
  18.5 1.4 fusion.22
  20.7 1.8 fusion.24
  26.0 1.7 multiply_reduce_fusion.3
  30.3 88.0 %all-reduce.4.cloned.1.call-done = f32[32,512]{1,0:T(8,128)} async-done(((f32[32,512]{1,0:T(8,128)}), f32[32,512]{1,0:T(8,128)}) %all-reduce.4.cloned.1.call-update) | async-done | bytes 65552 | tf_op jit(solution)/shard_map/psum | solution.py:105
  119.8 55.7 %all-gather.3.cloned.1.call-done = bf16[2048,2048]{1,0:T(8,128)(2,1)} async-done(((bf16[128,2048]{1,0:T(8,128)(2,1)}), bf16[2048,2048]{1,0:T(8,128)(2,1)}) %all-gather.3.cloned.1.call-update) | async-done | bytes 8388624 | tf_op jit(solution)/shard_map/all_gather | solution.py:120
  175.5 6.4 convolution_bitcast_fusion.1
  182.1 1.6 fusion.32
  183.9 2.7 convert_reduce_fusion.1
  186.6 2.1 fusion.37
  188.9 47.4 %psum.28 = f32[16,512]{1,0:T(8,128)} all-reduce(f32[16,512]{1,0:T(8,128)S(1)} %fusion.59), channel_id=1, replica_groups=mesh['sec'=2,'dp'=8,'seq'=16] {'seq'}, use_global_device_ids=true, to_apply=%region_10.11 | all-reduce | flops 8192 | bytes 65536 | tf_op jit(solution)/shard_map/psum | solution.py:144
  236.3 1.2 multiply_reduce_fusion.9
  237.5 1.0 fusion.45
  238.9 1.7 fusion.35
  241.6 1.0 copy-done.2
  244.9 8.1 convolution_bitcast_fusion
  253.3 100.3 %reduce-scatter.2.cloned.1.call-done = f32[1,128,2048]{2,1,0:T(8,128)} async-done(((f32[16,128,2048]{2,1,0:T(8,128)}), f32[1,128,2048]{2,1,0:T(8,128)}) %reduce-scatter.2.cloned.1.call-update) | async-done | bytes 1048592 | tf_op jit(solution)/shard_map/reduce_scatter | solution.py:186
  353.5 1.9 fusion.30
  355.7 2.1 multiply_reduce_fusion.7
  358.5 2.0 fusion.66
  360.9 2.7 fusion.27
  363.6 1.3 fusion.40
  365.0 1.0 scatter-add.10
  367.3 3.3 fusion.53
  370.6 1175.1 %all-reduce.6.cloned.1.call-done = f32[2560,256]{1,0:T(8,128)} async-done(((f32[2560,256]{1,0:T(8,128)}), f32[2560,256]{1,0:T(8,128)}) %all-reduce.6.cloned.1.call-update) | async-done | bytes 2621456 | tf_op jit(solution)/shard_map/psum | solution.py:15
  1546.5 3.2 fusion.18
  1549.6 1.5 reduce_sum.224
  1551.1 2.8 fusion.21
  1554.0 142.7 %all-reduce.8.cloned.1.call-done = f32[2560,256]{1,0:T(8,128)} async-done(((f32[2560,256]{1,0:T(8,128)}), f32[2560,256]{1,0:T(8,128)}) %all-reduce.8.cloned.1.call-update) | async-done | bytes 2621456 | tf_op jit(solution)/shard_map/psum | solution.py:16
  1696.7 1.6 constant_dynamic-slice_fusion
  (129 shorter events, 17.9 us)
Async XLA Ops:
  7.2 1.9 copy-start
  7.2 111.1 %all-reduce.4.cloned.1.call-start = ((), (), s32[]{:S(2)}) async-start(), calls=%async_computation.1 | async-start | bytes 131072 | tf_op jit(solution)/shard_map/psum | solution.py:105
  14.1 5.8 copy-start.20
  14.1 6.4 copy-start.21
  14.1 6.4 copy-start.22
  14.2 6.5 copy-start.36
  16.5 159.0 %all-gather.3.cloned.1.call-start = ((), (), s32[]{:S(2)}) async-start(), calls=%async_computation.5 | async-start | bytes 8912896 | tf_op jit(solution)/shard_map/all_gather | solution.py:120
  16.5 4.1 copy-start.3
  18.5 3.9 copy-start.23
  20.0 2.5 copy-start.27
  24.9 2.8 copy-start.10
  27.8 2.0 copy-start.37
  29.7 323.8 %reduce-scatter.2.cloned.1.call-start = ((), (), s32[]{:S(2)}) async-start(), calls=%async_computation.2 | async-start | bytes 17825792 | tf_op jit(solution)/shard_map/reduce_scatter | solution.py:186
  181.9 2.0 copy-start.1
  183.9 4.8 copy-start.13
  183.9 52.3 %copy-start.16 = (f32[32,512]{1,0:T(8,128)S(1)}, f32[32,512]{1,0:T(8,128)}, u32[]{:S(2)}) copy-start(f32[32,512]{1,0:T(8,128)} %all-reduce.4.cloned.1.call-done) | copy-start | bytes 196612
  236.3 4.4 copy-start.6
  237.5 3.5 copy-start.35
  238.5 2.5 copy-start.8
  240.6 1.9 copy-start.2
  253.0 100.5 %copy-start.26 = (f32[128]{0:T(128)S(1)}, f32[128]{0:T(128)}, u32[]{:S(2)}) copy-start(f32[128]{0:T(128)} %copy-done.25) | copy-start | bytes 1540
  253.0 102.5 %copy-start.18 = (f32[1,2048]{1,0:T(1,128)S(1)}, f32[1,2048]{1,0:T(1,128)}, u32[]{:S(2)}) copy-start(f32[1,2048]{1,0:T(1,128)} %get-tuple-element.66) | copy-start | bytes 24580
  253.0 102.5 %copy-start.19 = (f32[1,2048]{1,0:T(1,128)S(1)}, f32[1,2048]{1,0:T(1,128)}, u32[]{:S(2)}) copy-start(f32[1,2048]{1,0:T(1,128)} %get-tuple-element.67) | copy-start | bytes 24580
  253.1 1292.7 %all-reduce.6.cloned.1.call-start = ((), (), s32[]{:S(2)}) async-start(), calls=%async_computation.3 | async-start | bytes 5242880 | tf_op jit(solution)/shard_map/psum | solution.py:15
  353.5 2.0 copy-start.5
  353.5 2.2 copy-start.7
  355.7 2.7 copy-start.29
  355.7 2.7 copy-start.30
  355.7 2.7 copy-start.32
  355.7 2.7 copy-start.34
  355.7 5.0 copy-start.11
  370.6 1326.1 %all-reduce.8.cloned.1.call-start = ((), (), s32[]{:S(2)}) async-start(), calls=%async_computation.4 | async-start | bytes 5242880 | tf_op jit(solution)/shard_map/psum | solution.py:16
  (11 other events, 11.9 us)
Sparse Core Ops, SparseCore 0:
  16.6 101.6 all-reduce.3
  120.9 54.6 all-gather.2
  253.2 100.3 reduce-scatter.1
  370.7 1175.0 all-reduce.5
  1548.2 148.4 all-reduce.7
